TPU v7x, 256 devices: a whole 4x4x8 slice. The times are simulated.
256 devices in a mesh: row: 32 (over y, x, z_hi), col: 8 (over z_lo, core).
Axes of the slice: x: 4, y: 4, z: 8 (z_hi: 2, z_lo: 4; z = z_hi * 4 + z_lo), core: 2. Of those that a mesh axis runs over, the one named last changes fastest.
Arguments:
- rhs: float32 [32, 8, 12, 192, 128], P('row', 'col'), may hold values from -6 to 6
- smoother: bfloat16 [32, 8, 3, 3, 768], P('row', 'col'), may hold values from -0.375 to 2.375
- blocks: bfloat16 [32, 8, 12, 192, 1536], P('row', 'col'), may hold values from -0.15625 to 0.15625
- col_index: int32 [32, 8, 12, 8], P('row', 'col'), may hold values from 0 to 27, as said below
- send_list: int32 [32, 8, 4, 4], P('row', 'col'), may hold values from 0 to 11, as said below
- agg_id: int32 [32, 8, 12], P('row', 'col'), may hold values from 0 to 3, as said below
- prolong: bfloat16 [32, 8, 6, 2304], P('row', 'col'), may hold values from -0.4375 to 0.4375
- coarse_inverse: bfloat16 [6144, 6144], P('row'), may hold values from -0.078125 to 0.078125
Outputs:
- smoothed_solution: float32 [32, 8, 12, 192, 128], P('row', 'col')
Inputs may be any that keep to these rules, and one draw needn't show every extreme that they name: `col_index`: A value below 12 names a block row of the same device; the value 12 + 4 * g + j names slot j of ghost group g. Every ghost slot is named by some entry of each device. `send_list`: the 4 blocks of one device and group are distinct. `agg_id`: every aggregate of a device holds at least one block row.
All inputs are finite; a program needn't handle non-finite values.
Results may differ from a plain program's by a relative error of at most 0.0029.
Values may be sent and summed in bfloat16 or wider, within the bound.
No kernel may reach another device: no remote copies, remote signals or barrier semaphores. Data moves between devices by JAX's collectives and lax.ppermute only.
A program may use at most 64 MiB of HBM per device.

v0:
```python
import jax
import jax.numpy as jnp
from jax import lax
from jax.sharding import PartitionSpec as P

damping = 0.6


def passed_along(value, axis, steps):
    count = lax.axis_size(axis)
    pairs = [(source, (source + steps) % count) for source in range(count)]
    return lax.ppermute(value, axis, pairs)


def point_smooth(coefficients, vector):
    leading = vector.shape[:2]
    blocks = vector.shape[2]
    grains = vector.shape[3] // 3
    columns = vector.shape[4]
    factors = coefficients.astype(jnp.float32).reshape(leading + (3, 3, blocks, grains))
    pieces = vector.reshape(leading + (blocks, 3, grains, columns))
    outputs = []
    for component in range(3):
        summed = factors[:, :, component, 0, :, :, None] * pieces[:, :, :, 0]
        summed = summed + factors[:, :, component, 1, :, :, None] * pieces[:, :, :, 1]
        summed = summed + factors[:, :, component, 2, :, :, None] * pieces[:, :, :, 2]
        outputs.append(summed)
    return damping * jnp.stack(outputs, axis=3).reshape(vector.shape)


def body(rhs, smoother, blocks, col_index, send_list, agg_id, prolong, coarse_inverse):
    block_count = rhs.shape[2]
    dof_count = rhs.shape[3]
    vectors = rhs.shape[4]
    send_rows = send_list[0, 0]
    coarse_dofs = prolong.shape[2]
    shaped = prolong[0, 0].reshape((coarse_dofs, block_count, dof_count))

    def apply_operator(vector, ready_ghosts=None):
        vector_low = vector.astype(jnp.bfloat16)
        shard_low = vector_low[0, 0]
        ghosts = []
        for offset in (1, -1):
            packed = jnp.take(shard_low, send_rows[0 if offset == 1 else 1], axis=0)
            ghosts.append(passed_along(packed, "row", offset))
        for offset in (1, -1):
            packed = jnp.take(shard_low, send_rows[2 if offset == 1 else 3], axis=0)
            ghosts.append(passed_along(packed, "col", offset))
        source = jnp.concatenate([shard_low] + list(ghosts), axis=0)
        columns = col_index[0, 0]
        picked = jnp.take(source, columns.reshape(-1), axis=0).reshape((block_count, -1, vectors))
        product = jnp.einsum(
            "nde,ner->ndr", blocks[0, 0], picked, preferred_element_type=jnp.float32
        )
        return product[None, None]

    first_iter = point_smooth(smoother, rhs)
    residual_first = rhs - apply_operator(first_iter)
    update_second = point_smooth(smoother, residual_first)
    second_iter = first_iter + update_second
    residual_second = residual_first - apply_operator(update_second)
    coarse_rows = coarse_inverse.shape[1] // (lax.axis_size("row") * lax.axis_size("col"))
    aggregates = coarse_rows // coarse_dofs
    onehot = (agg_id[0, 0][None, :] == jnp.arange(aggregates, dtype=jnp.int32)[:, None]).astype(
        jnp.float32
    )
    local_terms = jnp.einsum(
        "knd,ndr->nkr",
        shaped,
        residual_second[0, 0].astype(jnp.bfloat16),
        preferred_element_type=jnp.float32,
    )
    coarse_residual = jnp.einsum(
        "an,nkr->akr", onehot, local_terms, precision=lax.Precision.HIGHEST
    )
    coarse_rhs = coarse_residual.astype(jnp.bfloat16).reshape((coarse_rows, vectors))
    column_place = lax.axis_index("col") * coarse_rows
    coarse_solution = jnp.dot(
        coarse_inverse,
        lax.all_gather(coarse_rhs, ("row", "col"), axis=0, tiled=True),
        preferred_element_type=jnp.float32,
    )
    coarse_solution = lax.dynamic_slice_in_dim(coarse_solution, column_place, coarse_rows, 0)
    coarse_rounded = coarse_solution.astype(jnp.bfloat16).reshape(
        (aggregates, coarse_dofs, vectors)
    )
    chosen = jnp.einsum(
        "an,akr->nkr",
        onehot.astype(jnp.bfloat16),
        coarse_rounded,
        preferred_element_type=jnp.float32,
    ).astype(jnp.bfloat16)
    correction = jnp.einsum("knd,nkr->ndr", shaped, chosen, preferred_element_type=jnp.float32)[
        None, None
    ]
    after_coarse = second_iter + correction
    residual_third = residual_second - apply_operator(correction)
    return after_coarse + point_smooth(smoother, residual_third)


def solution(mesh):
    placed = (
        P("row", "col", None, None, None),
        P("row", "col", None, None, None),
        P("row", "col", None, None, None),
        P("row", "col", None, None),
        P("row", "col", None, None),
        P("row", "col", None),
        P("row", "col", None, None),
        P("row", None),
    )
    return jax.shard_map(
        body,
        mesh=mesh,
        in_specs=placed,
        out_specs=P("row", "col", None, None, None),
        check_vma=False,
    )
```

profile of v0, /device:TPU:1, one launch (start us, length us, event | category | flops | bytes accessed | tf_op | source)
XLA Modules:
  0.0 296.1 jit_solution(9077023847655563413)
XLA Ops:
  6.5 1.5 compare_and_fusion.1
  9.5 2.9 multiply_add_fusion.8
  15.5 7.7 %collective-permute-start = (bf16[4,192,128]{2,1,0:T(8,128)(2,1)}, bf16[4,192,128]{2,1,0:T(8,128)(2,1)}, u32[]{:S(2)}, u32[]{:S(2)}) collective-permute-start(bf16[4,192,128]{2,1,0:T(8,128)(2,1)} %broadcast_select_fusion.14), channel_id=1, source_target_pairs={{0,8},{8,16},{16,24},{24,32},{32,40},{40,48},{48,56},{56,64},{64,7... | collective-permute-start | bytes 589832 | tf_op jit(solution)/shard_map/ppermute | solution.py:12
  26.6 4.6 %collective-permute-start.1 = (bf16[4,192,128]{2,1,0:T(8,128)(2,1)}, bf16[4,192,128]{2,1,0:T(8,128)(2,1)}, u32[]{:S(2)}, u32[]{:S(2)}) collective-permute-start(bf16[4,192,128]{2,1,0:T(8,128)(2,1)} %broadcast_select_fusion.11), channel_id=1, source_target_pairs={{0,248},{8,0},{16,8},{24,16},{32,24},{40,32},{48,40},{56,48},{64,5... | collective-permute-start | bytes 589832 | tf_op jit(solution)/shard_map/ppermute | solution.py:12
  34.5 1.6 collective-permute-start.2
  44.4 1.5 reshape_squeeze.9
  47.4 1.6 constant_dynamic-update-slice_fusion.3
  49.0 1.6 constant_dynamic-update-slice_fusion.2
  50.6 1.6 constant_dynamic-update-slice_fusion.1
  52.9 4.8 %gather_fusion.4 = bf16[96,192,128]{2,1,0:T(8,128)(2,1)} fusion(bf16[28,192,128]{2,1,0:T(8,128)(2,1)} %constant_dynamic-update-slice_fusion, s32[1024]{0:T(1024)S(1)} %pad_clamp_fusion), kind=kCustom, calls=%fused_computation.1.clone | custom fusion | bytes 9437568 | tf_op jit(solution)/shard_map/jit(_take)/gather | solution.py:51
  57.8 2.9 broadcast_select_fusion.2
  60.8 5.1 %fusion.15 = f32[1,1,12,192,128]{4,3,2,1,0:T(8,128)S(1)} fusion(f32[1,1,12,192,128]{4,3,2,1,0:T(8,128)S(1)} %copy-done.3, bf16[12,1536,128]{2,1,0:T(8,128)(2,1)S(1)} %bitcast.103, bf16[1,1,12,192,1536]{4,3,2,1,0:T(8,128)(2,1)} %param.14), kind=kOutput, calls=%fused_computation.28 | convolution fusion | flops 906264576 | bytes 14155776 | tf_op jit(solution)/shard_map/nde,ner->ndr/dot_general | solution.py:52
  76.5 8.7 %collective-permute-start.5 = (bf16[4,192,128]{2,1,0:T(8,128)(2,1)S(1)}, bf16[4,192,128]{2,1,0:T(8,128)(2,1)S(1)}, u32[]{:S(2)}, u32[]{:S(2)}) collective-permute-start(bf16[4,192,128]{2,1,0:T(8,128)(2,1)S(1)} %broadcast_select_fusion.10), channel_id=1, source_target_pairs={{0,248},{8,0},{16,8},{24,16},{32,24},{40,32},{48,40},{56,48},{64,5... | collective-permute-start | bytes 589832 | tf_op jit(solution)/shard_map/ppermute | solution.py:12
  85.2 2.3 collective-permute-start.6
  91.4 5.1 %collective-permute-done.6 = bf16[4,192,128]{2,1,0:T(8,128)(2,1)S(1)} collective-permute-done((bf16[4,192,128]{2,1,0:T(8,128)(2,1)S(1)}, bf16[4,192,128]{2,1,0:T(8,128)(2,1)S(1)}, u32[]{:S(2)}, u32[]{:S(2)}) %collective-permute-start.6) | collective-permute-done | bytes 196640 | tf_op jit(solution)/shard_map/ppermute | solution.py:12
  97.2 3.3 %collective-permute-done.7 = bf16[4,192,128]{2,1,0:T(8,128)(2,1)S(1)} collective-permute-done((bf16[4,192,128]{2,1,0:T(8,128)(2,1)S(1)}, bf16[4,192,128]{2,1,0:T(8,128)(2,1)S(1)}, u32[]{:S(2)}, u32[]{:S(2)}) %collective-permute-start.7) | collective-permute-done | bytes 196640 | tf_op jit(solution)/shard_map/ppermute | solution.py:12
  101.3 5.0 %gather_fusion.9 = bf16[96,192,128]{2,1,0:T(8,128)(2,1)} fusion(bf16[28,192,128]{2,1,0:T(8,128)(2,1)} %constant_dynamic-update-slice_fusion.5, s32[1024]{0:T(1024)} %copy-done.32), kind=kCustom, calls=%fused_computation.13.clone | custom fusion | bytes 9437568 | tf_op jit(solution)/shard_map/jit(_take)/gather | solution.py:51
  106.2 2.9 broadcast_select_fusion.1
  109.2 5.0 %fusion.18 = f32[1,1,12,192,128]{4,3,2,1,0:T(8,128)S(1)} fusion(f32[1,1,12,192,128]{4,3,2,1,0:T(8,128)S(1)} %copy-done.2, bf16[12,1536,128]{2,1,0:T(8,128)(2,1)S(1)} %bitcast.102, bf16[1,1,12,192,1536]{4,3,2,1,0:T(8,128)(2,1)} %param.14), kind=kOutput, calls=%fused_computation.29 | convolution fusion | flops 906264576 | bytes 14155776 | tf_op jit(solution)/shard_map/nde,ner->ndr/dot_general | solution.py:52
  116.5 102.9 %all-gather.2.cloned.1.call-done = bf16[6144,128]{1,0:T(8,128)(2,1)} async-done(((bf16[24,128]{1,0:T(8,128)(2,1)}), bf16[6144,128]{1,0:T(8,128)(2,1)}) %all-gather.2.cloned.1.call-update) | async-done | bytes 1572880 | tf_op jit(solution)/shard_map/all_gather | solution.py:80
  219.5 2.2 fusion.43
  224.5 2.6 constant_dynamic-update-slice_fusion.14
  227.1 2.4 gather_fusion.13
  229.5 2.4 gather_fusion.12
  232.0 2.4 gather_fusion.11
  234.4 2.5 gather_fusion.10
  239.9 7.6 %collective-permute-start.9 = (bf16[4,192,128]{2,1,0:T(8,128)(2,1)S(1)}, bf16[4,192,128]{2,1,0:T(8,128)(2,1)S(1)}, u32[]{:S(2)}, u32[]{:S(2)}) collective-permute-start(bf16[4,192,128]{2,1,0:T(8,128)(2,1)S(1)} %broadcast_select_fusion.9), channel_id=1, source_target_pairs={{0,248},{8,0},{16,8},{24,16},{32,24},{40,32},{48,40},{56,48},{64,5... | collective-permute-start | bytes 589832 | tf_op jit(solution)/shard_map/ppermute | solution.py:12
  248.5 1.7 collective-permute-start.10
  250.2 19.2 %collective-permute-done.8 = bf16[4,192,128]{2,1,0:T(8,128)(2,1)S(1)} collective-permute-done((bf16[4,192,128]{2,1,0:T(8,128)(2,1)S(1)}, bf16[4,192,128]{2,1,0:T(8,128)(2,1)S(1)}, u32[]{:S(2)}, u32[]{:S(2)}) %collective-permute-start.8) | collective-permute-done | bytes 196640 | tf_op jit(solution)/shard_map/ppermute | solution.py:12
  272.3 5.0 %gather_fusion.14 = bf16[96,192,128]{2,1,0:T(8,128)(2,1)} fusion(bf16[28,192,128]{2,1,0:T(8,128)(2,1)} %constant_dynamic-update-slice_fusion.10, s32[1024]{0:T(1024)} %copy-done.32), kind=kCustom, calls=%fused_computation.14.clone | custom fusion | bytes 9437568 | tf_op jit(solution)/shard_map/jit(_take)/gather | solution.py:51
  277.2 2.8 broadcast_select_fusion
  280.1 5.1 %fusion.21 = f32[1,1,12,192,128]{4,3,2,1,0:T(8,128)S(1)} fusion(f32[1,1,12,192,128]{4,3,2,1,0:T(8,128)S(1)} %fusion.18, bf16[12,1536,128]{2,1,0:T(8,128)(2,1)S(1)} %bitcast.101, bf16[1,1,12,192,1536]{4,3,2,1,0:T(8,128)(2,1)} %param.14), kind=kOutput, calls=%fused_computation.30 | convolution fusion | flops 906264576 | bytes 14155776 | tf_op jit(solution)/shard_map/nde,ner->ndr/dot_general | solution.py:52
  (143 shorter events, 53.4 us)
Async XLA Ops:
  6.5 213.0 %copy-start = (bf16[192,6144]{1,0:T(8,128)(2,1)S(1)}, bf16[192,6144]{1,0:T(8,128)(2,1)}, u32[]{:S(2)}) copy-start(bf16[192,6144]{1,0:T(8,128)(2,1)} %param.19) | copy-start | bytes 7077892
  6.5 212.9 %all-gather.2.cloned.1.call-start = ((), (), s32[]{:S(2)}) async-start(), calls=%async_computation | async-start | bytes 1579008 | tf_op jit(solution)/shard_map/all_gather | solution.py:80
  15.5 31.9 %collective-permute-start = (bf16[4,192,128]{2,1,0:T(8,128)(2,1)}, bf16[4,192,128]{2,1,0:T(8,128)(2,1)}, u32[]{:S(2)}, u32[]{:S(2)}) collective-permute-start(bf16[4,192,128]{2,1,0:T(8,128)(2,1)} %broadcast_select_fusion.14), channel_id=1, source_target_pairs={{0,8},{8,16},{16,24},{24,32},{32,40},{40,48},{48,56},{56,64},{64,7... | collective-permute-start | bytes 589832 | tf_op jit(solution)/shard_map/ppermute | solution.py:12
  26.6 22.4 %collective-permute-start.1 = (bf16[4,192,128]{2,1,0:T(8,128)(2,1)}, bf16[4,192,128]{2,1,0:T(8,128)(2,1)}, u32[]{:S(2)}, u32[]{:S(2)}) collective-permute-start(bf16[4,192,128]{2,1,0:T(8,128)(2,1)} %broadcast_select_fusion.11), channel_id=1, source_target_pairs={{0,248},{8,0},{16,8},{24,16},{32,24},{40,32},{48,40},{56,48},{64,5... | collective-permute-start | bytes 589832 | tf_op jit(solution)/shard_map/ppermute | solution.py:12
  34.5 16.1 %collective-permute-start.2 = (bf16[4,192,128]{2,1,0:T(8,128)(2,1)}, bf16[4,192,128]{2,1,0:T(8,128)(2,1)}, u32[]{:S(2)}, u32[]{:S(2)}) collective-permute-start(bf16[4,192,128]{2,1,0:T(8,128)(2,1)} %broadcast_select_fusion.8), channel_id=1, source_target_pairs={{0,1},{1,2},{2,3},{3,4},{4,5},{5,6},{6,7},{7,0},{8,9},{9,10},{10,1... | collective-permute-start | bytes 589832 | tf_op jit(solution)/shard_map/ppermute | solution.py:12
  39.4 12.8 %collective-permute-start.3 = (bf16[4,192,128]{2,1,0:T(8,128)(2,1)}, bf16[4,192,128]{2,1,0:T(8,128)(2,1)S(1)}, u32[]{:S(2)}, u32[]{:S(2)}) collective-permute-start(bf16[4,192,128]{2,1,0:T(8,128)(2,1)} %broadcast_select_fusion.5), channel_id=1, source_target_pairs={{0,7},{1,0},{2,1},{3,2},{4,3},{5,4},{6,5},{7,6},{8,15},{9,8},{10,9... | collective-permute-start | bytes 589832 | tf_op jit(solution)/shard_map/ppermute | solution.py:12
  47.4 10.4 %copy-start.32 = (s32[1024]{0:T(1024)}, s32[1024]{0:T(1024)S(1)}, u32[]{:S(2)}) copy-start(s32[1024]{0:T(1024)S(1)} %pad_clamp_fusion) | copy-start | bytes 12292
  60.7 5.2 %copy-start.12 = (f32[12,64]{1,0:T(8,128)S(1)}, f32[12,64]{1,0:T(8,128)}, u32[]{:S(2)}) copy-start(f32[12,64]{1,0:T(8,128)} %copy-done.11) | copy-start | bytes 9220
  60.7 5.2 %copy-start.15 = (f32[12,64]{1,0:T(8,128)S(1)}, f32[12,64]{1,0:T(8,128)}, u32[]{:S(2)}) copy-start(f32[12,64]{1,0:T(8,128)} %copy-done.14) | copy-start | bytes 9220
  60.7 5.2 %copy-start.18 = (f32[12,64]{1,0:T(8,128)S(1)}, f32[12,64]{1,0:T(8,128)}, u32[]{:S(2)}) copy-start(f32[12,64]{1,0:T(8,128)} %copy-done.17) | copy-start | bytes 9220
  60.7 5.2 %copy-start.21 = (f32[12,64]{1,0:T(8,128)S(1)}, f32[12,64]{1,0:T(8,128)}, u32[]{:S(2)}) copy-start(f32[12,64]{1,0:T(8,128)} %copy-done.20) | copy-start | bytes 9220
  60.8 5.2 %copy-start.24 = (f32[12,64]{1,0:T(8,128)S(1)}, f32[12,64]{1,0:T(8,128)}, u32[]{:S(2)}) copy-start(f32[12,64]{1,0:T(8,128)} %copy-done.23) | copy-start | bytes 9220
  60.8 5.2 %copy-start.27 = (f32[12,64]{1,0:T(8,128)S(1)}, f32[12,64]{1,0:T(8,128)}, u32[]{:S(2)}) copy-start(f32[12,64]{1,0:T(8,128)} %copy-done.26) | copy-start | bytes 9220
  60.8 5.2 %copy-start.30 = (f32[12,64]{1,0:T(8,128)S(1)}, f32[12,64]{1,0:T(8,128)}, u32[]{:S(2)}) copy-start(f32[12,64]{1,0:T(8,128)} %copy-done.29) | copy-start | bytes 9220
  74.7 14.9 %collective-permute-start.4 = (bf16[4,192,128]{2,1,0:T(8,128)(2,1)S(1)}, bf16[4,192,128]{2,1,0:T(8,128)(2,1)S(1)}, u32[]{:S(2)}, u32[]{:S(2)}) collective-permute-start(bf16[4,192,128]{2,1,0:T(8,128)(2,1)S(1)} %broadcast_select_fusion.13), channel_id=1, source_target_pairs={{0,8},{8,16},{16,24},{24,32},{32,40},{40,48},{48,56},{56,64},{64,7... | collective-permute-start | bytes 589832 | tf_op jit(solution)/shard_map/ppermute | solution.py:12
  76.5 14.2 %collective-permute-start.5 = (bf16[4,192,128]{2,1,0:T(8,128)(2,1)S(1)}, bf16[4,192,128]{2,1,0:T(8,128)(2,1)S(1)}, u32[]{:S(2)}, u32[]{:S(2)}) collective-permute-start(bf16[4,192,128]{2,1,0:T(8,128)(2,1)S(1)} %broadcast_select_fusion.10), channel_id=1, source_target_pairs={{0,248},{8,0},{16,8},{24,16},{32,24},{40,32},{48,40},{56,48},{64,5... | collective-permute-start | bytes 589832 | tf_op jit(solution)/shard_map/ppermute | solution.py:12
  85.2 11.4 %collective-permute-start.6 = (bf16[4,192,128]{2,1,0:T(8,128)(2,1)S(1)}, bf16[4,192,128]{2,1,0:T(8,128)(2,1)S(1)}, u32[]{:S(2)}, u32[]{:S(2)}) collective-permute-start(bf16[4,192,128]{2,1,0:T(8,128)(2,1)S(1)} %broadcast_select_fusion.7), channel_id=1, source_target_pairs={{0,1},{1,2},{2,3},{3,4},{4,5},{5,6},{6,7},{7,0},{8,9},{9,10},{10,1... | collective-permute-start | bytes 589832 | tf_op jit(solution)/shard_map/ppermute | solution.py:12
  87.5 13.1 %collective-permute-start.7 = (bf16[4,192,128]{2,1,0:T(8,128)(2,1)S(1)}, bf16[4,192,128]{2,1,0:T(8,128)(2,1)S(1)}, u32[]{:S(2)}, u32[]{:S(2)}) collective-permute-start(bf16[4,192,128]{2,1,0:T(8,128)(2,1)S(1)} %broadcast_select_fusion.4), channel_id=1, source_target_pairs={{0,7},{1,0},{2,1},{3,2},{4,3},{5,4},{6,5},{7,6},{8,15},{9,8},{10,9... | collective-permute-start | bytes 589832 | tf_op jit(solution)/shard_map/ppermute | solution.py:12
  101.3 5.0 %copy-start.34 = (pred[96]{0:T(512)(128)(4,1)S(1)}, pred[96]{0:T(512)(128)(4,1)}, u32[]{:S(2)}) copy-start(pred[96]{0:T(512)(128)(4,1)} %compare_and_fusion) | copy-start | bytes 292
  109.2 5.0 %copy-start.10 = (bf16[6,12,192]{2,1,0:T(8,128)(2,1)S(1)}, bf16[6,12,192]{2,1,0:T(8,128)(2,1)}, u32[]{:S(2)}) copy-start(bf16[6,12,192]{2,1,0:T(8,128)(2,1)} %reshape_squeeze.9) | copy-start | bytes 82948
  109.2 5.3 %copy-start.35 = (s32[1,1,12]{2,1,0:T(1,128)S(1)}, s32[1,1,12]{2,1,0:T(1,128)}, u32[]{:S(2)}) copy-start(s32[1,1,12]{2,1,0:T(1,128)} %param.17) | copy-start | bytes 148
  239.9 30.3 %collective-permute-start.9 = (bf16[4,192,128]{2,1,0:T(8,128)(2,1)S(1)}, bf16[4,192,128]{2,1,0:T(8,128)(2,1)S(1)}, u32[]{:S(2)}, u32[]{:S(2)}) collective-permute-start(bf16[4,192,128]{2,1,0:T(8,128)(2,1)S(1)} %broadcast_select_fusion.9), channel_id=1, source_target_pairs={{0,248},{8,0},{16,8},{24,16},{32,24},{40,32},{48,40},{56,48},{64,5... | collective-permute-start | bytes 589832 | tf_op jit(solution)/shard_map/ppermute | solution.py:12
  247.5 22.0 %collective-permute-start.8 = (bf16[4,192,128]{2,1,0:T(8,128)(2,1)S(1)}, bf16[4,192,128]{2,1,0:T(8,128)(2,1)S(1)}, u32[]{:S(2)}, u32[]{:S(2)}) collective-permute-start(bf16[4,192,128]{2,1,0:T(8,128)(2,1)S(1)} %broadcast_select_fusion.12), channel_id=1, source_target_pairs={{0,8},{8,16},{16,24},{24,32},{32,40},{40,48},{48,56},{56,64},{64,7... | collective-permute-start | bytes 589832 | tf_op jit(solution)/shard_map/ppermute | solution.py:12
  248.5 22.3 %collective-permute-start.10 = (bf16[4,192,128]{2,1,0:T(8,128)(2,1)S(1)}, bf16[4,192,128]{2,1,0:T(8,128)(2,1)S(1)}, u32[]{:S(2)}, u32[]{:S(2)}) collective-permute-start(bf16[4,192,128]{2,1,0:T(8,128)(2,1)S(1)} %broadcast_select_fusion.6), channel_id=1, source_target_pairs={{0,1},{1,2},{2,3},{3,4},{4,5},{5,6},{6,7},{7,0},{8,9},{9,10},{10,1... | collective-permute-start | bytes 589832 | tf_op jit(solution)/shard_map/ppermute | solution.py:12
  250.2 21.3 %collective-permute-start.11 = (bf16[4,192,128]{2,1,0:T(8,128)(2,1)S(1)}, bf16[4,192,128]{2,1,0:T(8,128)(2,1)S(1)}, u32[]{:S(2)}, u32[]{:S(2)}) collective-permute-start(bf16[4,192,128]{2,1,0:T(8,128)(2,1)S(1)} %broadcast_select_fusion.3), channel_id=1, source_target_pairs={{0,7},{1,0},{2,1},{3,2},{4,3},{5,4},{6,5},{7,6},{8,15},{9,8},{10,9... | collective-permute-start | bytes 589832 | tf_op jit(solution)/shard_map/ppermute | solution.py:12
  280.0 5.1 %copy-start.13 = (f32[12,64]{1,0:T(8,128)S(1)}, f32[12,64]{1,0:T(8,128)}, u32[]{:S(2)}) copy-start(f32[12,64]{1,0:T(8,128)} %copy-done.11) | copy-start | bytes 9220
  280.1 5.1 %copy-start.16 = (f32[12,64]{1,0:T(8,128)S(1)}, f32[12,64]{1,0:T(8,128)}, u32[]{:S(2)}) copy-start(f32[12,64]{1,0:T(8,128)} %copy-done.14) | copy-start | bytes 9220
  280.1 5.1 %copy-start.19 = (f32[12,64]{1,0:T(8,128)S(1)}, f32[12,64]{1,0:T(8,128)}, u32[]{:S(2)}) copy-start(f32[12,64]{1,0:T(8,128)} %copy-done.17) | copy-start | bytes 9220
  280.1 5.1 %copy-start.22 = (f32[12,64]{1,0:T(8,128)S(1)}, f32[12,64]{1,0:T(8,128)}, u32[]{:S(2)}) copy-start(f32[12,64]{1,0:T(8,128)} %copy-done.20) | copy-start | bytes 9220
  280.1 5.1 %copy-start.25 = (f32[12,64]{1,0:T(8,128)S(1)}, f32[12,64]{1,0:T(8,128)}, u32[]{:S(2)}) copy-start(f32[12,64]{1,0:T(8,128)} %copy-done.23) | copy-start | bytes 9220
  280.1 5.1 %copy-start.28 = (f32[12,64]{1,0:T(8,128)S(1)}, f32[12,64]{1,0:T(8,128)}, u32[]{:S(2)}) copy-start(f32[12,64]{1,0:T(8,128)} %copy-done.26) | copy-start | bytes 9220
  280.1 5.1 %copy-start.31 = (f32[12,64]{1,0:T(8,128)S(1)}, f32[12,64]{1,0:T(8,128)}, u32[]{:S(2)}) copy-start(f32[12,64]{1,0:T(8,128)} %copy-done.29) | copy-start | bytes 9220
  (17 other events, 48.2 us)
Sparse Core Ops, SparseCore 0:
  116.7 102.7 all-gather.1
where the time goes:
time: 297 us; the launch traced here: 296 us
  waiting for transfers between devices  131 us (44%)
  local copies, waits for them, and re-layouts  54.9 us (18%)
  other arithmetic  38.2 us (13%)
  starting transfers between devices  36.5 us (12%)
  matrix products  21.3 us (7%)
  between operations  14.1 us (5%)
    all_gather x1, waiting for transfers between devices, body(): lax.all_gather(coarse_rhs, ('row', 'col'), axis=0, tiled=True)  103 us
    ppermute x12, starting transfers between devices, passed_along(): return lax.ppermute(value, axis, pairs)  36.5 us
    ppermute x12, waiting for transfers between devices, passed_along(): return lax.ppermute(value, axis, pairs)  28.2 us
    dot_general x3, matrix products, apply_operator(): jnp.einsum('nde,ner->ndr', blocks[0, 0], picked, preferred_element_type=j...  15.1 us
    gather x3, local copies, waits for them, and re-layouts, apply_operator(): jnp.take(source, columns.reshape(-1), axis=0)  14.7 us
    unnamed x84, local copies, waits for them, and re-layouts  14.6 us
    select_n x4, other arithmetic, apply_operator(): jnp.take(source, columns.reshape(-1), axis=0)  9.78 us
    gather x6, local copies, waits for them, and re-layouts, apply_operator(): packed = jnp.take(shard_low, send_rows[2 if offset == 1 else 3], axis=0)  8.34 us
  transfers between devices with their start and end apart: 13, of which 5 were waited for; matrix products, arithmetic and copies ran while one was open for 10% of the time, Pallas kernels for 0%

commit v1 on v0

--- a/solution.py
+++ b/solution.py
@@ -77,7 +77,12 @@
     column_place = lax.axis_index("col") * coarse_rows
     coarse_solution = jnp.dot(
         coarse_inverse,
-        lax.all_gather(coarse_rhs, ("row", "col"), axis=0, tiled=True),
+        jnp.concatenate(
+            lax.all_to_all(
+                jnp.stack([coarse_rhs] * lax.axis_size(("row", "col"))), ("row", "col"), 0, 0
+            ),
+            axis=0,
+        ),
         preferred_element_type=jnp.float32,
     )
     coarse_solution = lax.dynamic_slice_in_dim(coarse_solution, column_place, coarse_rows, 0)

time: 297 us -> 231 us (0.78)
  waiting for transfers between devices: 131 us -> 67.3 us
  between operations: 14.1 us -> 0.69 us
  starting transfers between devices: 36.5 us -> 45.3 us
    all_gather x1 -> x0, waiting for transfers between devices: 103 us -> none  [body(): lax.all_gather(coarse_rhs, ('row', 'col'), axis=0, tiled=True)]
    all_to_all x0 -> x1, waiting for transfers between devices: none -> 42.9 us  [body(): lax.all_to_all(jnp.stack([coarse_rhs] * lax.axis_size(('row', 'col'))), (...]
    all_to_all x0 -> x1, starting transfers between devices: none -> 12.1 us  [body(): lax.all_to_all(jnp.stack([coarse_rhs] * lax.axis_size(('row', 'col'))), (...]
    ppermute x12, waiting for transfers between devices: 28.2 us -> 24.4 us  [passed_along(): return lax.ppermute(value, axis, pairs)]
    another operation x0 -> x2, local copies, waits for them, and re-layouts: none -> 3.37 us  [body(): jnp.stack([coarse_rhs] * lax.axis_size(('row', 'col')))]
    ppermute x12, starting transfers between devices: 36.5 us -> 33.2 us  [passed_along(): return lax.ppermute(value, axis, pairs)]
  transfers between devices with their start and end apart: 13 -> 13, of which waited for: 5 -> 7; matrix products, arithmetic and copies ran while one was open for 10% -> 13% of each run, Pallas kernels for 0% -> 0%
where the time goes in v1:
time: 231 us; the launch traced here: 230 us
  waiting for transfers between devices  67.3 us (29%)
  local copies, waits for them, and re-layouts  57 us (25%)
  starting transfers between devices  45.3 us (20%)
  other arithmetic  38 us (16%)
  matrix products  21.3 us (9%)
    all_to_all x1, waiting for transfers between devices, body(): lax.all_to_all(jnp.stack([coarse_rhs] * lax.axis_size(('row', 'col'))), (...  42.9 us
    ppermute x12, starting transfers between devices, passed_along(): return lax.ppermute(value, axis, pairs)  33.2 us
    ppermute x12, waiting for transfers between devices, passed_along(): return lax.ppermute(value, axis, pairs)  24.4 us
    dot_general x3, matrix products, apply_operator(): jnp.einsum('nde,ner->ndr', blocks[0, 0], picked, preferred_element_type=j...  15.1 us
    gather x3, local copies, waits for them, and re-layouts, apply_operator(): jnp.take(source, columns.reshape(-1), axis=0)  14.8 us
    unnamed x84, local copies, waits for them, and re-layouts  14.7 us
    all_to_all x1, starting transfers between devices, body(): lax.all_to_all(jnp.stack([coarse_rhs] * lax.axis_size(('row', 'col'))), (...  12.1 us
    select_n x4, other arithmetic, apply_operator(): jnp.take(source, columns.reshape(-1), axis=0)  9.71 us
  transfers between devices with their start and end apart: 13, of which 7 were waited for; matrix products, arithmetic and copies ran while one was open for 13% of the time, Pallas kernels for 0%

profile of v1, /device:TPU:1, one launch (start us, length us, event | category | flops | bytes accessed | tf_op | source)
XLA Modules:
  0.0 229.6 jit_solution(2443327972444680252)
XLA Ops:
  3.0 2.9 %multiply_add_fusion.8 = (f32[1,1,12,1,64,128]{5,4,3,2,1,0:T(8,128)S(1)}, f32[1,1,12,1,64,128]{5,4,3,2,1,0:T(8,128)S(1)}, f32[1,1,12,1,64,128]{5,4,3,2,1,0:T(8,128)S(1)}) fusion(f32[1,1,12,3,64,128]{5,4,3,2,1,0:T(8,128)} %bitcast.106, f32[12,64]{1,0:T(8,128)S(1)} %get-tuple-element.35, f32[12,64]{1,0:T(8,128)S(1)} %get-tuple-element.36, ...), kind=kLoop, calls=%fused_computation.50 | loop fusion | flops 1474560 | bytes 2386944 | tf_op jit(solution)/shard_map/add | solution.py:26
  9.0 7.7 %collective-permute-start = (bf16[4,192,128]{2,1,0:T(8,128)(2,1)}, bf16[4,192,128]{2,1,0:T(8,128)(2,1)}, u32[]{:S(2)}, u32[]{:S(2)}) collective-permute-start(bf16[4,192,128]{2,1,0:T(8,128)(2,1)} %broadcast_select_fusion.14), channel_id=1, source_target_pairs={{0,8},{8,16},{16,24},{24,32},{32,40},{40,48},{48,56},{56,64},{64,7... | collective-permute-start | bytes 589832 | tf_op jit(solution)/shard_map/ppermute | solution.py:12
  20.1 4.6 %collective-permute-start.1 = (bf16[4,192,128]{2,1,0:T(8,128)(2,1)}, bf16[4,192,128]{2,1,0:T(8,128)(2,1)}, u32[]{:S(2)}, u32[]{:S(2)}) collective-permute-start(bf16[4,192,128]{2,1,0:T(8,128)(2,1)} %broadcast_select_fusion.11), channel_id=1, source_target_pairs={{0,248},{8,0},{16,8},{24,16},{32,24},{40,32},{48,40},{56,48},{64,5... | collective-permute-start | bytes 589832 | tf_op jit(solution)/shard_map/ppermute | solution.py:12
  40.6 1.6 constant_dynamic-update-slice_fusion.3
  42.2 1.6 constant_dynamic-update-slice_fusion.2
  43.9 1.6 constant_dynamic-update-slice_fusion.1
  46.2 4.8 %gather_fusion.4 = bf16[96,192,128]{2,1,0:T(8,128)(2,1)} fusion(bf16[28,192,128]{2,1,0:T(8,128)(2,1)} %constant_dynamic-update-slice_fusion, s32[1024]{0:T(1024)S(1)} %pad_clamp_fusion), kind=kCustom, calls=%fused_computation.1.clone | custom fusion | bytes 9437568 | tf_op jit(solution)/shard_map/jit(_take)/gather | solution.py:51
  51.0 2.9 %broadcast_select_fusion.2 = bf16[96,192,128]{2,1,0:T(8,128)(2,1)S(1)} fusion(bf16[96,192,128]{2,1,0:T(8,128)(2,1)} %gather_fusion.4, pred[96]{0:T(512)(128)(4,1)S(1)} %copy-done.33), kind=kLoop, calls=%fused_computation.23 | loop fusion | flops 2359296 | bytes 9437280 | tf_op jit(solution)/shard_map/jit(_take)/select_n | solution.py:51
  54.0 5.1 %fusion.15 = f32[1,1,12,192,128]{4,3,2,1,0:T(8,128)S(1)} fusion(f32[1,1,12,192,128]{4,3,2,1,0:T(8,128)S(1)} %copy-done.3, bf16[12,1536,128]{2,1,0:T(8,128)(2,1)S(1)} %bitcast.104, bf16[1,1,12,192,1536]{4,3,2,1,0:T(8,128)(2,1)} %param.14), kind=kOutput, calls=%fused_computation.28 | convolution fusion | flops 906264576 | bytes 14155776 | tf_op jit(solution)/shard_map/nde,ner->ndr/dot_general | solution.py:52
  69.7 8.7 %collective-permute-start.5 = (bf16[4,192,128]{2,1,0:T(8,128)(2,1)S(1)}, bf16[4,192,128]{2,1,0:T(8,128)(2,1)S(1)}, u32[]{:S(2)}, u32[]{:S(2)}) collective-permute-start(bf16[4,192,128]{2,1,0:T(8,128)(2,1)S(1)} %broadcast_select_fusion.10), channel_id=1, source_target_pairs={{0,248},{8,0},{16,8},{24,16},{32,24},{40,32},{48,40},{56,48},{64,5... | collective-permute-start | bytes 589832 | tf_op jit(solution)/shard_map/ppermute | solution.py:12
  78.4 2.3 %collective-permute-start.6 = (bf16[4,192,128]{2,1,0:T(8,128)(2,1)S(1)}, bf16[4,192,128]{2,1,0:T(8,128)(2,1)S(1)}, u32[]{:S(2)}, u32[]{:S(2)}) collective-permute-start(bf16[4,192,128]{2,1,0:T(8,128)(2,1)S(1)} %broadcast_select_fusion.7), channel_id=1, source_target_pairs={{0,1},{1,2},{2,3},{3,4},{4,5},{5,6},{6,7},{7,0},{8,9},{9,10},{10,1... | collective-permute-start | bytes 589832 | tf_op jit(solution)/shard_map/ppermute | solution.py:12
  84.6 5.1 %collective-permute-done.6 = bf16[4,192,128]{2,1,0:T(8,128)(2,1)S(1)} collective-permute-done((bf16[4,192,128]{2,1,0:T(8,128)(2,1)S(1)}, bf16[4,192,128]{2,1,0:T(8,128)(2,1)S(1)}, u32[]{:S(2)}, u32[]{:S(2)}) %collective-permute-start.6) | collective-permute-done | bytes 196640 | tf_op jit(solution)/shard_map/ppermute | solution.py:12
  90.5 3.3 %collective-permute-done.7 = bf16[4,192,128]{2,1,0:T(8,128)(2,1)S(1)} collective-permute-done((bf16[4,192,128]{2,1,0:T(8,128)(2,1)S(1)}, bf16[4,192,128]{2,1,0:T(8,128)(2,1)S(1)}, u32[]{:S(2)}, u32[]{:S(2)}) %collective-permute-start.7) | collective-permute-done | bytes 196640 | tf_op jit(solution)/shard_map/ppermute | solution.py:12
  94.4 5.0 %gather_fusion.9 = bf16[96,192,128]{2,1,0:T(8,128)(2,1)} fusion(bf16[28,192,128]{2,1,0:T(8,128)(2,1)} %constant_dynamic-update-slice_fusion.5, s32[1024]{0:T(1024)} %copy-done.32), kind=kCustom, calls=%fused_computation.13.clone | custom fusion | bytes 9437568 | tf_op jit(solution)/shard_map/jit(_take)/gather | solution.py:51
  99.4 2.9 %broadcast_select_fusion.1 = bf16[96,192,128]{2,1,0:T(8,128)(2,1)S(1)} fusion(bf16[96,192,128]{2,1,0:T(8,128)(2,1)} %gather_fusion.9, pred[96]{0:T(512)(128)(4,1)S(1)} %copy-done.34), kind=kLoop, calls=%fused_computation.22 | loop fusion | flops 2359296 | bytes 9437280 | tf_op jit(solution)/shard_map/jit(_take)/select_n | solution.py:51
  102.4 5.0 %fusion.18 = f32[1,1,12,192,128]{4,3,2,1,0:T(8,128)S(1)} fusion(f32[1,1,12,192,128]{4,3,2,1,0:T(8,128)S(1)} %copy-done.2, bf16[12,1536,128]{2,1,0:T(8,128)(2,1)S(1)} %bitcast.103, bf16[1,1,12,192,1536]{4,3,2,1,0:T(8,128)(2,1)} %param.14), kind=kOutput, calls=%fused_computation.29 | convolution fusion | flops 906264576 | bytes 14155776 | tf_op jit(solution)/shard_map/nde,ner->ndr/dot_general | solution.py:52
  109.7 2.1 stack.10
  111.8 12.1 %all-to-all-start = ((bf16[256,24,128]{2,1,0:T(8,128)(2,1)}), bf16[256,24,128]{2,1,0:T(8,128)(2,1)}, u32[]{:S(2)}, u32[]{:S(2)}) async-start(bf16[256,24,128]{2,1,0:T(8,128)(2,1)} %stack.10), calls=%async_computation | async-start | bytes 3145728 | tf_op jit(solution)/shard_map/all_to_all | solution.py:81
  123.9 42.9 %all-to-all-done = bf16[256,24,128]{2,1,0:T(8,128)(2,1)} async-done(((bf16[256,24,128]{2,1,0:T(8,128)(2,1)}), bf16[256,24,128]{2,1,0:T(8,128)(2,1)}, u32[]{:S(2)}, u32[]{:S(2)}) %all-to-all-start) | async-done | bytes 1572896 | tf_op jit(solution)/shard_map/all_to_all | solution.py:81
  166.8 2.2 fusion.43
  171.8 2.7 %constant_dynamic-update-slice_fusion.14 = (bf16[28,192,128]{2,1,0:T(8,128)(2,1)}, bf16[12,192,128]{2,1,0:T(8,128)(2,1)}, f32[12,192,128]{2,1,0:T(8,128)}) fusion(bf16[6,12,192]{2,1,0:T(8,128)(2,1)} %reshape_squeeze.9, bf16[12,6,128]{2,0,1:T(8,128)(2,1)S(1)} %fusion.35), kind=kOutput, calls=%fused_computation.82 | convolution fusion | flops 3833855 | bytes 2405376 | tf_op jit(solution)/shard_map/knd,nkr->ndr/dot_general | solution.py:98
  174.4 2.4 %gather_fusion.13 = bf16[4,192,128]{2,1,0:T(8,128)(2,1)} fusion(bf16[12,192,128]{2,1,0:T(8,128)(2,1)} %get-tuple-element.8, s32[1024]{0:T(1024)} %pad_clamp_fusion.1), kind=kCustom, calls=%fused_computation.12.clone | custom fusion | bytes 393232 | tf_op jit(solution)/shard_map/jit(_take)/gather | solution.py:47
  176.9 2.4 %gather_fusion.12 = bf16[4,192,128]{2,1,0:T(8,128)(2,1)} fusion(bf16[12,192,128]{2,1,0:T(8,128)(2,1)} %get-tuple-element.8, s32[1024]{0:T(1024)} %pad_clamp_fusion.2), kind=kCustom, calls=%fused_computation.11.clone | custom fusion | bytes 393232 | tf_op jit(solution)/shard_map/jit(_take)/gather | solution.py:47
  179.3 2.4 %gather_fusion.11 = bf16[4,192,128]{2,1,0:T(8,128)(2,1)} fusion(bf16[12,192,128]{2,1,0:T(8,128)(2,1)} %get-tuple-element.8, s32[1024]{0:T(1024)} %pad_clamp_fusion.3), kind=kCustom, calls=%fused_computation.10.clone | custom fusion | bytes 393232 | tf_op jit(solution)/shard_map/jit(_take)/gather | solution.py:44
  181.7 2.5 %gather_fusion.10 = bf16[4,192,128]{2,1,0:T(8,128)(2,1)} fusion(bf16[12,192,128]{2,1,0:T(8,128)(2,1)} %get-tuple-element.8, s32[1024]{0:T(1024)} %pad_clamp_fusion.4), kind=kCustom, calls=%fused_computation.9.clone | custom fusion | bytes 393232 | tf_op jit(solution)/shard_map/jit(_take)/gather | solution.py:44
  187.2 2.1 collective-permute-start.9
  189.3 3.4 %collective-permute-start.8 = (bf16[4,192,128]{2,1,0:T(8,128)(2,1)S(1)}, bf16[4,192,128]{2,1,0:T(8,128)(2,1)S(1)}, u32[]{:S(2)}, u32[]{:S(2)}) collective-permute-start(bf16[4,192,128]{2,1,0:T(8,128)(2,1)S(1)} %broadcast_select_fusion.12), channel_id=1, source_target_pairs={{0,8},{8,16},{16,24},{24,32},{32,40},{40,48},{48,56},{56,64},{64,7... | collective-permute-start | bytes 589832 | tf_op jit(solution)/shard_map/ppermute | solution.py:12
  194.3 11.2 %collective-permute-done.8 = bf16[4,192,128]{2,1,0:T(8,128)(2,1)S(1)} collective-permute-done((bf16[4,192,128]{2,1,0:T(8,128)(2,1)S(1)}, bf16[4,192,128]{2,1,0:T(8,128)(2,1)S(1)}, u32[]{:S(2)}, u32[]{:S(2)}) %collective-permute-start.8) | collective-permute-done | bytes 196640 | tf_op jit(solution)/shard_map/ppermute | solution.py:12
  206.9 3.6 %collective-permute-done.10 = bf16[4,192,128]{2,1,0:T(8,128)(2,1)S(1)} collective-permute-done((bf16[4,192,128]{2,1,0:T(8,128)(2,1)S(1)}, bf16[4,192,128]{2,1,0:T(8,128)(2,1)S(1)}, u32[]{:S(2)}, u32[]{:S(2)}) %collective-permute-start.10) | collective-permute-done | bytes 196640 | tf_op jit(solution)/shard_map/ppermute | solution.py:12
  212.5 5.0 %gather_fusion.14 = bf16[96,192,128]{2,1,0:T(8,128)(2,1)} fusion(bf16[28,192,128]{2,1,0:T(8,128)(2,1)} %constant_dynamic-update-slice_fusion.10, s32[1024]{0:T(1024)} %copy-done.32), kind=kCustom, calls=%fused_computation.14.clone | custom fusion | bytes 9437568 | tf_op jit(solution)/shard_map/jit(_take)/gather | solution.py:51
  217.5 2.8 %broadcast_select_fusion = bf16[96,192,128]{2,1,0:T(8,128)(2,1)S(1)} fusion(bf16[96,192,128]{2,1,0:T(8,128)(2,1)} %gather_fusion.14, pred[96]{0:T(512)(128)(4,1)} %compare_and_fusion), kind=kLoop, calls=%fused_computation.21 | loop fusion | flops 2359296 | bytes 9437280 | tf_op jit(solution)/shard_map/jit(_take)/select_n | solution.py:51
  220.4 5.1 %fusion.21 = f32[1,1,12,192,128]{4,3,2,1,0:T(8,128)S(1)} fusion(f32[1,1,12,192,128]{4,3,2,1,0:T(8,128)S(1)} %fusion.18, bf16[12,1536,128]{2,1,0:T(8,128)(2,1)S(1)} %bitcast.102, bf16[1,1,12,192,1536]{4,3,2,1,0:T(8,128)(2,1)} %param.14), kind=kOutput, calls=%fused_computation.30 | convolution fusion | flops 906264576 | bytes 14155776 | tf_op jit(solution)/shard_map/nde,ner->ndr/dot_general | solution.py:52
  (143 shorter events, 58.9 us)
Async XLA Ops:
  0.0 166.8 %copy-start = (bf16[192,6144]{1,0:T(8,128)(2,1)S(1)}, bf16[192,6144]{1,0:T(8,128)(2,1)}, u32[]{:S(2)}) copy-start(bf16[192,6144]{1,0:T(8,128)(2,1)} %param.19) | copy-start | bytes 7077892
  9.0 31.6 %collective-permute-start = (bf16[4,192,128]{2,1,0:T(8,128)(2,1)}, bf16[4,192,128]{2,1,0:T(8,128)(2,1)}, u32[]{:S(2)}, u32[]{:S(2)}) collective-permute-start(bf16[4,192,128]{2,1,0:T(8,128)(2,1)} %broadcast_select_fusion.14), channel_id=1, source_target_pairs={{0,8},{8,16},{16,24},{24,32},{32,40},{40,48},{48,56},{56,64},{64,7... | collective-permute-start | bytes 589832 | tf_op jit(solution)/shard_map/ppermute | solution.py:12
  20.1 22.2 %collective-permute-start.1 = (bf16[4,192,128]{2,1,0:T(8,128)(2,1)}, bf16[4,192,128]{2,1,0:T(8,128)(2,1)}, u32[]{:S(2)}, u32[]{:S(2)}) collective-permute-start(bf16[4,192,128]{2,1,0:T(8,128)(2,1)} %broadcast_select_fusion.11), channel_id=1, source_target_pairs={{0,248},{8,0},{16,8},{24,16},{32,24},{40,32},{48,40},{56,48},{64,5... | collective-permute-start | bytes 589832 | tf_op jit(solution)/shard_map/ppermute | solution.py:12
  28.0 15.9 %collective-permute-start.2 = (bf16[4,192,128]{2,1,0:T(8,128)(2,1)}, bf16[4,192,128]{2,1,0:T(8,128)(2,1)}, u32[]{:S(2)}, u32[]{:S(2)}) collective-permute-start(bf16[4,192,128]{2,1,0:T(8,128)(2,1)} %broadcast_select_fusion.8), channel_id=1, source_target_pairs={{0,1},{1,2},{2,3},{3,4},{4,5},{5,6},{6,7},{7,0},{8,9},{9,10},{10,1... | collective-permute-start | bytes 589832 | tf_op jit(solution)/shard_map/ppermute | solution.py:12
  32.8 12.6 %collective-permute-start.3 = (bf16[4,192,128]{2,1,0:T(8,128)(2,1)}, bf16[4,192,128]{2,1,0:T(8,128)(2,1)S(1)}, u32[]{:S(2)}, u32[]{:S(2)}) collective-permute-start(bf16[4,192,128]{2,1,0:T(8,128)(2,1)} %broadcast_select_fusion.5), channel_id=1, source_target_pairs={{0,7},{1,0},{2,1},{3,2},{4,3},{5,4},{6,5},{7,6},{8,15},{9,8},{10,9... | collective-permute-start | bytes 589832 | tf_op jit(solution)/shard_map/ppermute | solution.py:12
  40.6 10.4 %copy-start.32 = (s32[1024]{0:T(1024)}, s32[1024]{0:T(1024)S(1)}, u32[]{:S(2)}) copy-start(s32[1024]{0:T(1024)S(1)} %pad_clamp_fusion) | copy-start | bytes 12292
  54.0 5.2 %copy-start.12 = (f32[12,64]{1,0:T(8,128)S(1)}, f32[12,64]{1,0:T(8,128)}, u32[]{:S(2)}) copy-start(f32[12,64]{1,0:T(8,128)} %copy-done.11) | copy-start | bytes 9220
  54.0 5.2 %copy-start.15 = (f32[12,64]{1,0:T(8,128)S(1)}, f32[12,64]{1,0:T(8,128)}, u32[]{:S(2)}) copy-start(f32[12,64]{1,0:T(8,128)} %copy-done.14) | copy-start | bytes 9220
  54.0 5.2 %copy-start.18 = (f32[12,64]{1,0:T(8,128)S(1)}, f32[12,64]{1,0:T(8,128)}, u32[]{:S(2)}) copy-start(f32[12,64]{1,0:T(8,128)} %copy-done.17) | copy-start | bytes 9220
  54.0 5.2 %copy-start.21 = (f32[12,64]{1,0:T(8,128)S(1)}, f32[12,64]{1,0:T(8,128)}, u32[]{:S(2)}) copy-start(f32[12,64]{1,0:T(8,128)} %copy-done.20) | copy-start | bytes 9220
  54.0 5.2 %copy-start.24 = (f32[12,64]{1,0:T(8,128)S(1)}, f32[12,64]{1,0:T(8,128)}, u32[]{:S(2)}) copy-start(f32[12,64]{1,0:T(8,128)} %copy-done.23) | copy-start | bytes 9220
  54.0 5.2 %copy-start.27 = (f32[12,64]{1,0:T(8,128)S(1)}, f32[12,64]{1,0:T(8,128)}, u32[]{:S(2)}) copy-start(f32[12,64]{1,0:T(8,128)} %copy-done.26) | copy-start | bytes 9220
  54.0 5.2 %copy-start.30 = (f32[12,64]{1,0:T(8,128)S(1)}, f32[12,64]{1,0:T(8,128)}, u32[]{:S(2)}) copy-start(f32[12,64]{1,0:T(8,128)} %copy-done.29) | copy-start | bytes 9220
  67.9 14.9 %collective-permute-start.4 = (bf16[4,192,128]{2,1,0:T(8,128)(2,1)S(1)}, bf16[4,192,128]{2,1,0:T(8,128)(2,1)S(1)}, u32[]{:S(2)}, u32[]{:S(2)}) collective-permute-start(bf16[4,192,128]{2,1,0:T(8,128)(2,1)S(1)} %broadcast_select_fusion.13), channel_id=1, source_target_pairs={{0,8},{8,16},{16,24},{24,32},{32,40},{40,48},{48,56},{56,64},{64,7... | collective-permute-start | bytes 589832 | tf_op jit(solution)/shard_map/ppermute | solution.py:12
  69.7 14.2 %collective-permute-start.5 = (bf16[4,192,128]{2,1,0:T(8,128)(2,1)S(1)}, bf16[4,192,128]{2,1,0:T(8,128)(2,1)S(1)}, u32[]{:S(2)}, u32[]{:S(2)}) collective-permute-start(bf16[4,192,128]{2,1,0:T(8,128)(2,1)S(1)} %broadcast_select_fusion.10), channel_id=1, source_target_pairs={{0,248},{8,0},{16,8},{24,16},{32,24},{40,32},{48,40},{56,48},{64,5... | collective-permute-start | bytes 589832 | tf_op jit(solution)/shard_map/ppermute | solution.py:12
  78.4 11.4 %collective-permute-start.6 = (bf16[4,192,128]{2,1,0:T(8,128)(2,1)S(1)}, bf16[4,192,128]{2,1,0:T(8,128)(2,1)S(1)}, u32[]{:S(2)}, u32[]{:S(2)}) collective-permute-start(bf16[4,192,128]{2,1,0:T(8,128)(2,1)S(1)} %broadcast_select_fusion.7), channel_id=1, source_target_pairs={{0,1},{1,2},{2,3},{3,4},{4,5},{5,6},{6,7},{7,0},{8,9},{9,10},{10,1... | collective-permute-start | bytes 589832 | tf_op jit(solution)/shard_map/ppermute | solution.py:12
  80.7 13.0 %collective-permute-start.7 = (bf16[4,192,128]{2,1,0:T(8,128)(2,1)S(1)}, bf16[4,192,128]{2,1,0:T(8,128)(2,1)S(1)}, u32[]{:S(2)}, u32[]{:S(2)}) collective-permute-start(bf16[4,192,128]{2,1,0:T(8,128)(2,1)S(1)} %broadcast_select_fusion.4), channel_id=1, source_target_pairs={{0,7},{1,0},{2,1},{3,2},{4,3},{5,4},{6,5},{7,6},{8,15},{9,8},{10,9... | collective-permute-start | bytes 589832 | tf_op jit(solution)/shard_map/ppermute | solution.py:12
  94.4 5.0 %copy-start.34 = (pred[96]{0:T(512)(128)(4,1)S(1)}, pred[96]{0:T(512)(128)(4,1)}, u32[]{:S(2)}) copy-start(pred[96]{0:T(512)(128)(4,1)} %compare_and_fusion) | copy-start | bytes 292
  102.3 5.0 %copy-start.10 = (bf16[6,12,192]{2,1,0:T(8,128)(2,1)S(1)}, bf16[6,12,192]{2,1,0:T(8,128)(2,1)}, u32[]{:S(2)}) copy-start(bf16[6,12,192]{2,1,0:T(8,128)(2,1)} %reshape_squeeze.9) | copy-start | bytes 82948
  102.3 5.3 %copy-start.35 = (s32[1,1,12]{2,1,0:T(1,128)S(1)}, s32[1,1,12]{2,1,0:T(1,128)}, u32[]{:S(2)}) copy-start(s32[1,1,12]{2,1,0:T(1,128)} %param.17) | copy-start | bytes 148
  111.8 55.0 %all-to-all-start = ((bf16[256,24,128]{2,1,0:T(8,128)(2,1)}), bf16[256,24,128]{2,1,0:T(8,128)(2,1)}, u32[]{:S(2)}, u32[]{:S(2)}) async-start(bf16[256,24,128]{2,1,0:T(8,128)(2,1)} %stack.10), calls=%async_computation | async-start | bytes 3145728 | tf_op jit(solution)/shard_map/all_to_all | solution.py:81
  187.2 19.0 %collective-permute-start.9 = (bf16[4,192,128]{2,1,0:T(8,128)(2,1)S(1)}, bf16[4,192,128]{2,1,0:T(8,128)(2,1)S(1)}, u32[]{:S(2)}, u32[]{:S(2)}) collective-permute-start(bf16[4,192,128]{2,1,0:T(8,128)(2,1)S(1)} %broadcast_select_fusion.9), channel_id=1, source_target_pairs={{0,248},{8,0},{16,8},{24,16},{32,24},{40,32},{48,40},{56,48},{64,5... | collective-permute-start | bytes 589832 | tf_op jit(solution)/shard_map/ppermute | solution.py:12
  189.3 16.2 %collective-permute-start.8 = (bf16[4,192,128]{2,1,0:T(8,128)(2,1)S(1)}, bf16[4,192,128]{2,1,0:T(8,128)(2,1)S(1)}, u32[]{:S(2)}, u32[]{:S(2)}) collective-permute-start(bf16[4,192,128]{2,1,0:T(8,128)(2,1)S(1)} %broadcast_select_fusion.12), channel_id=1, source_target_pairs={{0,8},{8,16},{16,24},{24,32},{32,40},{40,48},{48,56},{56,64},{64,7... | collective-permute-start | bytes 589832 | tf_op jit(solution)/shard_map/ppermute | solution.py:12
  193.7 16.8 %collective-permute-start.10 = (bf16[4,192,128]{2,1,0:T(8,128)(2,1)S(1)}, bf16[4,192,128]{2,1,0:T(8,128)(2,1)S(1)}, u32[]{:S(2)}, u32[]{:S(2)}) collective-permute-start(bf16[4,192,128]{2,1,0:T(8,128)(2,1)S(1)} %broadcast_select_fusion.6), channel_id=1, source_target_pairs={{0,1},{1,2},{2,3},{3,4},{4,5},{5,6},{6,7},{7,0},{8,9},{9,10},{10,1... | collective-permute-start | bytes 589832 | tf_op jit(solution)/shard_map/ppermute | solution.py:12
  193.8 18.0 %collective-permute-start.11 = (bf16[4,192,128]{2,1,0:T(8,128)(2,1)S(1)}, bf16[4,192,128]{2,1,0:T(8,128)(2,1)S(1)}, u32[]{:S(2)}, u32[]{:S(2)}) collective-permute-start(bf16[4,192,128]{2,1,0:T(8,128)(2,1)S(1)} %broadcast_select_fusion.3), channel_id=1, source_target_pairs={{0,7},{1,0},{2,1},{3,2},{4,3},{5,4},{6,5},{7,6},{8,15},{9,8},{10,9... | collective-permute-start | bytes 589832 | tf_op jit(solution)/shard_map/ppermute | solution.py:12
  220.3 5.1 %copy-start.13 = (f32[12,64]{1,0:T(8,128)S(1)}, f32[12,64]{1,0:T(8,128)}, u32[]{:S(2)}) copy-start(f32[12,64]{1,0:T(8,128)} %copy-done.11) | copy-start | bytes 9220
  220.3 5.1 %copy-start.16 = (f32[12,64]{1,0:T(8,128)S(1)}, f32[12,64]{1,0:T(8,128)}, u32[]{:S(2)}) copy-start(f32[12,64]{1,0:T(8,128)} %copy-done.14) | copy-start | bytes 9220
  220.3 5.1 %copy-start.19 = (f32[12,64]{1,0:T(8,128)S(1)}, f32[12,64]{1,0:T(8,128)}, u32[]{:S(2)}) copy-start(f32[12,64]{1,0:T(8,128)} %copy-done.17) | copy-start | bytes 9220
  220.3 5.1 %copy-start.22 = (f32[12,64]{1,0:T(8,128)S(1)}, f32[12,64]{1,0:T(8,128)}, u32[]{:S(2)}) copy-start(f32[12,64]{1,0:T(8,128)} %copy-done.20) | copy-start | bytes 9220
  220.4 5.1 %copy-start.25 = (f32[12,64]{1,0:T(8,128)S(1)}, f32[12,64]{1,0:T(8,128)}, u32[]{:S(2)}) copy-start(f32[12,64]{1,0:T(8,128)} %copy-done.23) | copy-start | bytes 9220
  220.4 5.1 %copy-start.28 = (f32[12,64]{1,0:T(8,128)S(1)}, f32[12,64]{1,0:T(8,128)}, u32[]{:S(2)}) copy-start(f32[12,64]{1,0:T(8,128)} %copy-done.26) | copy-start | bytes 9220
  220.4 5.1 %copy-start.31 = (f32[12,64]{1,0:T(8,128)S(1)}, f32[12,64]{1,0:T(8,128)}, u32[]{:S(2)}) copy-start(f32[12,64]{1,0:T(8,128)} %copy-done.29) | copy-start | bytes 9220
  (17 other events, 48.2 us)
